TPU v7x, 32 devices: a whole 2x2x4 slice. The times are simulated.
32 devices in a mesh: grad: 4 (over y, x), col: 8 (over z, core).
Axes of the slice: x: 2, y: 2, z: 4, core: 2. Of those that a mesh axis runs over, the one named last changes fastest.
Arguments:
- gradient: bfloat16 [16384, 53248], P(('grad', 'col'))
- test_matrix: bfloat16 [16384, 256], P(('grad', 'col')), may hold values from -6 to 6
Outputs:
- low_rank: float32 [16384, 256], P(('grad', 'col'))
- projector: float32 [53248, 256], P('col')
All inputs are finite; a program needn't handle non-finite values.
Results may differ from a plain program's by a relative error of at most 0.008.
Values may be sent and summed in bfloat16 or wider, within the bound.
No kernel may reach another device: no remote copies, remote signals or barrier semaphores. Data moves between devices by JAX's collectives and lax.ppermute only.
A program may use at most 256 MiB of HBM per device.

v0:
```python
import math
import jax
import jax.numpy as jnp
from jax import lax
from jax.sharding import PartitionSpec as P

FF = 53248
POWER = 2


def orthonormal(matrix, reduce_gram):
    partial_gram = lax.dot_general(
        matrix,
        matrix,
        (((0,), (0,)), ((), ())),
        precision=lax.Precision.HIGHEST,
        preferred_element_type=jnp.float32,
    )
    gram = reduce_gram(partial_gram)
    lower_factor = jnp.linalg.cholesky(gram)
    return lax.linalg.triangular_solve(
        lower_factor, matrix, left_side=False, lower=True, transpose_a=True
    )


def gram_over_columns(partial_gram):
    return lax.psum(partial_gram, "col")


def shards(gradient, test_matrix):
    blocks = lax.all_to_all(gradient, "col", split_axis=1, concat_axis=0, tiled=True)

    def add_sketch(row_piece):
        return lax.dot_general(
            blocks, row_piece, (((0,), (0,)), ((), ())), preferred_element_type=jnp.float32
        )

    sketch = add_sketch(lax.all_gather(test_matrix, "col", axis=0, tiled=True))
    for iteration in range(POWER + 1):
        summed = lax.psum(sketch, "grad")
        basis_block = orthonormal(summed, gram_over_columns)
        basis_bf = basis_block.astype(jnp.bfloat16)
        reduced = lax.psum_scatter(
            jnp.dot(blocks, basis_bf, preferred_element_type=jnp.float32),
            "col",
            scatter_dimension=0,
            tiled=True,
        )
        if iteration < POWER:
            reduced_bf = reduced.astype(jnp.bfloat16)
            sketch = add_sketch(lax.all_gather(reduced_bf, "col", axis=0, tiled=True))
    return (reduced, basis_block * math.sqrt(FF))


def solution(mesh):
    return jax.shard_map(
        shards,
        mesh=mesh,
        in_specs=(P(("grad", "col"), None), P(("grad", "col"), None)),
        out_specs=(P(("grad", "col"), None), P("col", None)),
        check_vma=False,
    )
```

profile of v0, /device:TPU:0, one launch (start us, length us, event | category | flops | bytes accessed | tf_op | source)
XLA Modules:
  0.0 2602.8 jit_solution(11232503956803364355)
XLA Ops:
  7.2 70.6 %copy.20 = bf16[512,53248]{0,1:T(8,128)(2,1)} copy(bf16[512,53248]{1,0:T(8,128)(2,1)} %param.5) | data formatting | bytes 109051904 | tf_op args[0]
  87.4 1189.5 %all-to-all-done = bf16[512,8,6656]{0,2,1:T(8,128)(2,1)} async-done(((bf16[512,8,6656]{0,2,1:T(8,128)(2,1)}), bf16[512,8,6656]{0,2,1:T(8,128)(2,1)}, u32[]{:S(2)}, u32[]{:S(2)}) %all-to-all-start) | async-done | bytes 54525984 | tf_op jit(solution)/shard_map/all_to_all | solution.py:31
  1276.9 64.6 %copy.21 = bf16[8,512,6656]{2,1,0:T(8,128)(2,1)} copy(bf16[8,512,6656]{1,2,0:T(8,128)(2,1)} %bitcast.1) | data formatting | bytes 109051904 | tf_op jit(solution)/shard_map/all_to_all | solution.py:31
  1341.5 25.8 fusion.41
  1367.7 146.1 %all-reduce.8.cloned.1.call-done = f32[6656,256]{1,0:T(8,128)} async-done(((f32[6656,256]{1,0:T(8,128)}), f32[6656,256]{1,0:T(8,128)}) %all-reduce.8.cloned.1.call-update) | async-done | bytes 6815760 | tf_op jit(solution)/shard_map/psum | solution.py:40
  1513.8 16.6 fusion.42
  1531.0 55.0 %all-reduce.10.cloned.1.call-done = f32[256,256]{0,1:T(8,128)} async-done(((f32[256,256]{0,1:T(8,128)}), f32[256,256]{0,1:T(8,128)}) %all-reduce.10.cloned.1.call-update) | async-done | bytes 262160 | tf_op jit(solution)/shard_map/psum | solution.py:27
  1588.1 11.7 cholesky.172
  1610.2 11.7 cholesky.189
  1628.9 19.7 custom-call.16
  1664.7 24.3 convolution_bitcast_fusion.4
  1689.1 49.1 %reduce-scatter.4.cloned.1.call-done = f32[512,256]{0,1:T(8,128)} async-done(((f32[4096,256]{0,1:T(8,128)}), f32[512,256]{0,1:T(8,128)}) %reduce-scatter.4.cloned.1.call-update) | async-done | bytes 524304 | tf_op jit(solution)/shard_map/reduce_scatter | solution.py:43
  1740.1 27.8 %all-gather.6.cloned.1.call-done = bf16[4096,256]{0,1:T(8,128)(2,1)} async-done(((bf16[512,256]{0,1:T(8,128)(2,1)}), bf16[4096,256]{0,1:T(8,128)(2,1)}) %all-gather.6.cloned.1.call-update) | async-done | bytes 2097168 | tf_op jit(solution)/shard_map/all_gather | solution.py:51
  1767.9 25.5 convolution_bitcast_fusion.1
  1793.5 146.3 %all-reduce.12.cloned.1.call-done = f32[6656,256]{0,1:T(8,128)} async-done(((f32[6656,256]{0,1:T(8,128)}), f32[6656,256]{0,1:T(8,128)}) %all-reduce.12.cloned.1.call-update) | async-done | bytes 6815760 | tf_op jit(solution)/shard_map/psum | solution.py:40
  1939.8 19.3 fusion.43
  1959.6 55.1 %all-reduce.14.cloned.1.call-done = f32[256,256]{0,1:T(8,128)} async-done(((f32[256,256]{0,1:T(8,128)}), f32[256,256]{0,1:T(8,128)}) %all-reduce.14.cloned.1.call-update) | async-done | bytes 262160 | tf_op jit(solution)/shard_map/psum | solution.py:27
  2016.8 11.7 cholesky.206
  2038.9 11.7 cholesky.223
  2058.1 19.7 custom-call.18
  2091.4 24.5 convolution_bitcast_fusion.3
  2116.0 49.1 %reduce-scatter.6.cloned.1.call-done = f32[512,256]{0,1:T(8,128)} async-done(((f32[4096,256]{0,1:T(8,128)}), f32[512,256]{0,1:T(8,128)}) %reduce-scatter.6.cloned.1.call-update) | async-done | bytes 524304 | tf_op jit(solution)/shard_map/reduce_scatter | solution.py:43
  2167.0 28.0 %all-gather.8.cloned.1.call-done = bf16[4096,256]{0,1:T(8,128)(2,1)} async-done(((bf16[512,256]{0,1:T(8,128)(2,1)}), bf16[4096,256]{0,1:T(8,128)(2,1)}) %all-gather.8.cloned.1.call-update) | async-done | bytes 2097168 | tf_op jit(solution)/shard_map/all_gather | solution.py:51
  2194.9 25.5 convolution_bitcast_fusion
  2220.5 146.3 %all-reduce.16.cloned.1.call-done = f32[6656,256]{0,1:T(8,128)} async-done(((f32[6656,256]{0,1:T(8,128)}), f32[6656,256]{0,1:T(8,128)}) %all-reduce.16.cloned.1.call-update) | async-done | bytes 6815760 | tf_op jit(solution)/shard_map/psum | solution.py:40
  2366.8 19.3 fusion.44
  2386.6 55.1 %all-reduce.18.cloned.1.call-done = f32[256,256]{0,1:T(8,128)} async-done(((f32[256,256]{0,1:T(8,128)}), f32[256,256]{0,1:T(8,128)}) %all-reduce.18.cloned.1.call-update) | async-done | bytes 262160 | tf_op jit(solution)/shard_map/psum | solution.py:27
  2443.9 11.7 cholesky.240
  2465.9 11.7 cholesky.257
  2485.2 19.7 custom-call.20
  2519.2 25.4 convolution_bitcast_fusion.2
  2558.0 35.7 %reduce-scatter.8.cloned.1.call-done = f32[512,256]{0,1:T(8,128)} async-done(((f32[4096,256]{0,1:T(8,128)}), f32[512,256]{0,1:T(8,128)}) %reduce-scatter.8.cloned.1.call-update) | async-done | bytes 524304 | tf_op jit(solution)/shard_map/reduce_scatter | solution.py:43
  (113 shorter events, 142.1 us)
Async XLA Ops:
  77.8 1199.1 %all-to-all-start = ((bf16[512,8,6656]{0,2,1:T(8,128)(2,1)}), bf16[512,8,6656]{0,2,1:T(8,128)(2,1)}, u32[]{:S(2)}, u32[]{:S(2)}) async-start(bf16[512,8,6656]{0,2,1:T(8,128)(2,1)} %bitcast.124), calls=%async_computation | async-start | bytes 109051904 | tf_op jit(solution)/shard_map/all_to_all | solution.py:31
  86.6 1254.9 %all-gather.4.cloned.1.call-start = ((), (), s32[]{:S(2)}) async-start(), calls=%async_computation.4 | async-start | bytes 2359296 | tf_op jit(solution)/shard_map/all_gather | solution.py:38
  87.3 1426.5 %all-reduce.8.cloned.1.call-start = ((), (), s32[]{:S(2)}) async-start(), calls=%async_computation.5 | async-start | bytes 13631488 | tf_op jit(solution)/shard_map/psum | solution.py:40
  1367.4 218.6 %all-reduce.10.cloned.1.call-start = ((), (), s32[]{:S(2)}) async-start(), calls=%async_computation.6 | async-start | bytes 524288 | tf_op jit(solution)/shard_map/psum | solution.py:27
  1530.4 207.8 %reduce-scatter.4.cloned.1.call-start = ((), (), s32[]{:S(2)}) async-start(), calls=%async_computation.7 | async-start | bytes 4718592 | tf_op jit(solution)/shard_map/reduce_scatter | solution.py:43
  1628.2 0.7 copy-start.4
  1648.5 5.2 copy-start
  1689.1 78.8 %all-gather.6.cloned.1.call-start = ((), (), s32[]{:S(2)}) async-start(), calls=%async_computation.8 | async-start | bytes 2359296 | tf_op jit(solution)/shard_map/all_gather | solution.py:51
  1740.0 199.8 %all-reduce.12.cloned.1.call-start = ((), (), s32[]{:S(2)}) async-start(), calls=%async_computation.9 | async-start | bytes 13631488 | tf_op jit(solution)/shard_map/psum | solution.py:40
  1793.4 221.3 %all-reduce.14.cloned.1.call-start = ((), (), s32[]{:S(2)}) async-start(), calls=%async_computation.10 | async-start | bytes 524288 | tf_op jit(solution)/shard_map/psum | solution.py:27
  1959.1 206.0 %reduce-scatter.6.cloned.1.call-start = ((), (), s32[]{:S(2)}) async-start(), calls=%async_computation.11 | async-start | bytes 4718592 | tf_op jit(solution)/shard_map/reduce_scatter | solution.py:43
  2057.4 0.7 copy-start.5
  2077.8 5.2 copy-start.2
  2116.0 79.0 %all-gather.8.cloned.1.call-start = ((), (), s32[]{:S(2)}) async-start(), calls=%async_computation.12 | async-start | bytes 2359296 | tf_op jit(solution)/shard_map/all_gather | solution.py:51
  2166.9 199.9 %all-reduce.16.cloned.1.call-start = ((), (), s32[]{:S(2)}) async-start(), calls=%async_computation.13 | async-start | bytes 13631488 | tf_op jit(solution)/shard_map/psum | solution.py:40
  2220.5 221.3 %all-reduce.18.cloned.1.call-start = ((), (), s32[]{:S(2)}) async-start(), calls=%async_computation.14 | async-start | bytes 524288 | tf_op jit(solution)/shard_map/psum | solution.py:27
  2386.2 207.5 %reduce-scatter.8.cloned.1.call-start = ((), (), s32[]{:S(2)}) async-start(), calls=%async_computation.15 | async-start | bytes 4718592 | tf_op jit(solution)/shard_map/reduce_scatter | solution.py:43
  2484.5 0.7 copy-start.3
  2504.9 5.2 copy-start.1
Sparse Core Ops, SparseCore 0:
  89.0 49.5 all-gather.3
  1367.5 146.2 all-reduce.7
  1530.6 55.4 all-reduce.9
  1689.2 48.9 reduce-scatter.3
  1740.2 27.5 all-gather.5
  1793.5 146.1 all-reduce.11
  1959.2 55.4 all-reduce.13
  2116.1 48.9 reduce-scatter.5
  2167.3 27.6 all-gather.7
  2220.6 146.1 all-reduce.15
  2386.3 55.4 all-reduce.17
  2544.7 48.9 reduce-scatter.7
where the time goes:
time: 2610 us; the launch traced here: 2600 us
  waiting for transfers between devices  1980 us (76%)
  matrix products  252 us (10%)
  other arithmetic  174 us (7%)
  local copies, waits for them, and re-layouts  163 us (6%)
    all_to_all x1, waiting for transfers between devices, shards(): lax.all_to_all(gradient, 'col', split_axis=1, concat_axis=0, tiled=True)  1190 us
    psum x3, waiting for transfers between devices, shards(): summed = lax.psum(sketch, 'grad')  439 us
    psum x3, waiting for transfers between devices, gram_over_columns(): return lax.psum(partial_gram, 'col')  165 us
    reduce_scatter x3, waiting for transfers between devices, shards(): lax.psum_scatter(jnp.dot(blocks, basis_bf, preferred_element_type=jnp.flo...  134 us
    another operation x20, other arithmetic, orthonormal(): lower_factor = jnp.linalg.cholesky(gram)  103 us
    unnamed x15, local copies, waits for them, and re-layouts  82.9 us
    dot_general x3, matrix products, add_sketch(): lax.dot_general(blocks, row_piece, (((0,), (0,)), ((), ())), preferred_el...  76.9 us
    dot_general x3, matrix products, shards(): jnp.dot(blocks, basis_bf, preferred_element_type=jnp.float32)  74.2 us
  transfers between devices with their start and end apart: 13, of which 12 were waited for; matrix products, arithmetic and copies ran while one was open for 3% of the time, Pallas kernels for 0%

commit v1 on v0

--- a/solution.py
+++ b/solution.py
@@ -37,7 +37,17 @@
 
     sketch = add_sketch(lax.all_gather(test_matrix, "col", axis=0, tiled=True))
     for iteration in range(POWER + 1):
-        summed = lax.psum(sketch, "grad")
+
+        def _show_sources_all(field_in):
+            axis_total = lax.axis_size("grad")
+            parts_out = field_in
+            for k0 in [d for d in (1, 2, 4, 8, 16) if d < axis_total]:
+                parts_out = parts_out + lax.ppermute(
+                    parts_out, "grad", tuple(((s, s ^ k0) for s in range(axis_total)))
+                )
+            return parts_out
+
+        summed = _show_sources_all(sketch)
         basis_block = orthonormal(summed, gram_over_columns)
         basis_bf = basis_block.astype(jnp.bfloat16)
         reduced = lax.psum_scatter(

time: 2610 us -> 3060 us (1.17)
  waiting for transfers between devices: 1980 us -> 2420 us
    ppermute x0 -> x6, waiting for transfers between devices: none -> 881 us  [_show_sources_all(): lax.ppermute(parts_out, 'grad', tuple(((s, s ^ k0) for s in range(axis_to...]
    psum x3 -> x0, waiting for transfers between devices: 439 us -> none  [shards(): summed = lax.psum(sketch, 'grad')]
    unnamed x15 -> x29, local copies, waits for them, and re-layouts: 82.9 us -> 91.2 us
  transfers between devices with their start and end apart: 13 -> 16, of which waited for: 12 -> 15; matrix products, arithmetic and copies ran while one was open for 3% -> 3% of each run, Pallas kernels for 0% -> 0%
where the time goes in v1:
time: 3060 us; the launch traced here: 3050 us
  waiting for transfers between devices  2420 us (79%)
  matrix products  224 us (7%)
  other arithmetic  198 us (6%)
  local copies, waits for them, and re-layouts  171 us (6%)
    all_to_all x1, waiting for transfers between devices, shards(): lax.all_to_all(gradient, 'col', split_axis=1, concat_axis=0, tiled=True)  1190 us
    ppermute x6, waiting for transfers between devices, _show_sources_all(): lax.ppermute(parts_out, 'grad', tuple(((s, s ^ k0) for s in range(axis_to...  881 us
    psum x3, waiting for transfers between devices, gram_over_columns(): return lax.psum(partial_gram, 'col')  165 us
    reduce_scatter x3, waiting for transfers between devices, shards(): lax.psum_scatter(jnp.dot(blocks, basis_bf, preferred_element_type=jnp.flo...  132 us
    another operation x20, other arithmetic, orthonormal(): lower_factor = jnp.linalg.cholesky(gram)  103 us
    unnamed x29, local copies, waits for them, and re-layouts  91.2 us
    dot_general x3, matrix products, add_sketch(): lax.dot_general(blocks, row_piece, (((0,), (0,)), ((), ())), preferred_el...  78.4 us
    dot_general x3, matrix products, shards(): jnp.dot(blocks, basis_bf, preferred_element_type=jnp.float32)  77 us
  transfers between devices with their start and end apart: 16, of which 15 were waited for; matrix products, arithmetic and copies ran while one was open for 3% of the time, Pallas kernels for 0%

profile of v1, /device:TPU:0, one launch (start us, length us, event | category | flops | bytes accessed | tf_op | source)
XLA Modules:
  0.0 3054.8 jit_solution(4228706518478287738)
XLA Ops:
  7.2 70.5 %copy.20 = bf16[512,53248]{0,1:T(8,128)(2,1)} copy(bf16[512,53248]{1,0:T(8,128)(2,1)} %param.5) | data formatting | bytes 109051904 | tf_op args[0]
  87.2 1189.5 %all-to-all-done = bf16[512,8,6656]{0,2,1:T(8,128)(2,1)} async-done(((bf16[512,8,6656]{0,2,1:T(8,128)(2,1)}), bf16[512,8,6656]{0,2,1:T(8,128)(2,1)}, u32[]{:S(2)}, u32[]{:S(2)}) %all-to-all-start) | async-done | bytes 54525984 | tf_op jit(solution)/shard_map/all_to_all | solution.py:31
  1276.7 64.7 %copy.21 = bf16[8,512,6656]{2,1,0:T(8,128)(2,1)} copy(bf16[8,512,6656]{1,2,0:T(8,128)(2,1)} %bitcast.1) | data formatting | bytes 109051904 | tf_op jit(solution)/shard_map/all_to_all | solution.py:31
  1341.4 26.2 fusion.44
  1369.8 146.7 %collective-permute-done = f32[6656,256]{1,0:T(8,128)S(1)} collective-permute-done((f32[6656,256]{1,0:T(8,128)}, f32[6656,256]{1,0:T(8,128)S(1)}, u32[]{:S(2)}, u32[]{:S(2)}) %collective-permute-start) | collective-permute-done | bytes 6815776 | tf_op jit(solution)/shard_map/ppermute | solution.py:45
  1522.2 146.0 %collective-permute-done.1 = f32[6656,256]{1,0:T(8,128)} collective-permute-done((f32[6656,256]{1,0:T(8,128)S(1)}, f32[6656,256]{1,0:T(8,128)}, u32[]{:S(2)}, u32[]{:S(2)}) %collective-permute-start.1) | collective-permute-done | bytes 6815776 | tf_op jit(solution)/shard_map/ppermute | solution.py:45
  1674.8 12.2 fusion.45
  1687.1 55.4 %all-reduce.5.cloned.1.call-done = f32[256,256]{0,1:T(8,128)} async-done(((f32[256,256]{0,1:T(8,128)}), f32[256,256]{0,1:T(8,128)}) %all-reduce.5.cloned.1.call-update) | async-done | bytes 262160 | tf_op jit(solution)/shard_map/psum | solution.py:27
  1744.6 11.7 cholesky.172
  1766.7 11.7 cholesky.189
  1784.5 19.7 custom-call.16
  1819.5 25.5 convolution_bitcast_fusion.4
  1845.0 49.1 %reduce-scatter.4.cloned.1.call-done = f32[512,256]{0,1:T(8,128)} async-done(((f32[4096,256]{0,1:T(8,128)}), f32[512,256]{0,1:T(8,128)}) %reduce-scatter.4.cloned.1.call-update) | async-done | bytes 524304 | tf_op jit(solution)/shard_map/reduce_scatter | solution.py:53
  1896.0 27.8 all-gather.6.cloned.1.call-done
  1923.8 26.1 convolution_bitcast_fusion.1
  1951.4 147.6 %collective-permute-done.2 = f32[6656,256]{0,1:T(8,128)S(1)} collective-permute-done((f32[6656,256]{0,1:T(8,128)}, f32[6656,256]{0,1:T(8,128)S(1)}, u32[]{:S(2)}, u32[]{:S(2)}) %collective-permute-start.2) | collective-permute-done | bytes 6815776 | tf_op jit(solution)/shard_map/ppermute | solution.py:45
  2104.6 146.7 %collective-permute-done.3 = f32[6656,256]{0,1:T(8,128)} collective-permute-done((f32[6656,256]{0,1:T(8,128)S(1)}, f32[6656,256]{0,1:T(8,128)}, u32[]{:S(2)}, u32[]{:S(2)}) %collective-permute-start.3) | collective-permute-done | bytes 6815776 | tf_op jit(solution)/shard_map/ppermute | solution.py:45
  2264.6 54.8 %all-reduce.7.cloned.1.call-done = f32[256,256]{0,1:T(8,128)} async-done(((f32[256,256]{0,1:T(8,128)}), f32[256,256]{0,1:T(8,128)}) %all-reduce.7.cloned.1.call-update) | async-done | bytes 262160 | tf_op jit(solution)/shard_map/psum | solution.py:27
  2321.5 11.7 cholesky.206
  2343.5 11.7 cholesky.223
  2361.9 19.7 custom-call.18
  2394.6 25.5 convolution_bitcast_fusion.3
  2420.2 49.1 %reduce-scatter.6.cloned.1.call-done = f32[512,256]{0,1:T(8,128)} async-done(((f32[4096,256]{0,1:T(8,128)}), f32[512,256]{0,1:T(8,128)}) %reduce-scatter.6.cloned.1.call-update) | async-done | bytes 524304 | tf_op jit(solution)/shard_map/reduce_scatter | solution.py:53
  2471.1 28.0 all-gather.8.cloned.1.call-done
  2499.1 26.1 convolution_bitcast_fusion
  2526.7 147.6 %collective-permute-done.4 = f32[6656,256]{0,1:T(8,128)S(1)} collective-permute-done((f32[6656,256]{0,1:T(8,128)}, f32[6656,256]{0,1:T(8,128)S(1)}, u32[]{:S(2)}, u32[]{:S(2)}) %collective-permute-start.4) | collective-permute-done | bytes 6815776 | tf_op jit(solution)/shard_map/ppermute | solution.py:45
  2679.9 146.7 %collective-permute-done.5 = f32[6656,256]{0,1:T(8,128)} collective-permute-done((f32[6656,256]{0,1:T(8,128)S(1)}, f32[6656,256]{0,1:T(8,128)}, u32[]{:S(2)}, u32[]{:S(2)}) %collective-permute-start.5) | collective-permute-done | bytes 6815776 | tf_op jit(solution)/shard_map/ppermute | solution.py:45
  2840.0 54.8 %all-reduce.9.cloned.1.call-done = f32[256,256]{0,1:T(8,128)} async-done(((f32[256,256]{0,1:T(8,128)}), f32[256,256]{0,1:T(8,128)}) %all-reduce.9.cloned.1.call-update) | async-done | bytes 262160 | tf_op jit(solution)/shard_map/psum | solution.py:27
  2918.9 11.7 cholesky.257
  2937.3 19.7 custom-call.20
  2970.8 26.1 convolution_bitcast_fusion.2
  3012.3 33.7 %reduce-scatter.8.cloned.1.call-done = f32[512,256]{0,1:T(8,128)} async-done(((f32[4096,256]{0,1:T(8,128)}), f32[512,256]{0,1:T(8,128)}) %reduce-scatter.8.cloned.1.call-update) | async-done | bytes 524304 | tf_op jit(solution)/shard_map/reduce_scatter | solution.py:53
  (139 shorter events, 204.2 us)
Async XLA Ops:
  77.6 1199.1 %all-to-all-start = ((bf16[512,8,6656]{0,2,1:T(8,128)(2,1)}), bf16[512,8,6656]{0,2,1:T(8,128)(2,1)}, u32[]{:S(2)}, u32[]{:S(2)}) async-start(bf16[512,8,6656]{0,2,1:T(8,128)(2,1)} %bitcast.121), calls=%async_computation | async-start | bytes 109051904 | tf_op jit(solution)/shard_map/all_to_all | solution.py:31
  86.5 1255.0 %all-gather.4.cloned.1.call-start = ((), (), s32[]{:S(2)}) async-start(), calls=%async_computation.4 | async-start | bytes 2359296 | tf_op jit(solution)/shard_map/all_gather | solution.py:38
  87.2 1655.3 %all-reduce.5.cloned.1.call-start = ((), (), s32[]{:S(2)}) async-start(), calls=%async_computation.5 | async-start | bytes 524288 | tf_op jit(solution)/shard_map/psum | solution.py:27
  1367.6 148.9 %collective-permute-start = (f32[6656,256]{1,0:T(8,128)}, f32[6656,256]{1,0:T(8,128)S(1)}, u32[]{:S(2)}, u32[]{:S(2)}) collective-permute-start(f32[6656,256]{1,0:T(8,128)} %fusion.44), channel_id=1, source_target_pairs={{0,8},{8,0},{16,24},{24,16},{1,9},{9,1},{17,25},{25,17},{2,10},{10... | collective-permute-start | bytes 20447240 | tf_op jit(solution)/shard_map/ppermute | solution.py:45
  1520.3 147.8 %collective-permute-start.1 = (f32[6656,256]{1,0:T(8,128)S(1)}, f32[6656,256]{1,0:T(8,128)}, u32[]{:S(2)}, u32[]{:S(2)}) collective-permute-start(f32[6656,256]{1,0:T(8,128)S(1)} %add.47), channel_id=1, source_target_pairs={{0,16},{8,24},{16,0},{24,8},{1,17},{9,25},{17,1},{25,9},{2,18},{10... | collective-permute-start | bytes 20447240 | tf_op jit(solution)/shard_map/ppermute | solution.py:45
  1671.9 2.9 copy-start
  1687.1 207.0 %reduce-scatter.4.cloned.1.call-start = ((), (), s32[]{:S(2)}) async-start(), calls=%async_computation.6 | async-start | bytes 4718592 | tf_op jit(solution)/shard_map/reduce_scatter | solution.py:53
  1780.4 34.6 %slice-start = ((s8[6815744]{0:T(1024)(128)(4,1)}), s8[2621440]{0:T(1024)(128)(4,1)S(1)}, s32[]{:S(2)}) async-start(s8[6815744]{0:T(1024)(128)(4,1)} %bitcast.122), calls=%async_computation.13 | async-start | bytes 5242880
  1804.2 10.9 slice-start.1
  1809.6 9.9 copy-start.5
  1845.0 78.8 %all-gather.6.cloned.1.call-start = ((), (), s32[]{:S(2)}) async-start(), calls=%async_computation.7 | async-start | bytes 2359296 | tf_op jit(solution)/shard_map/all_gather | solution.py:61
  1895.9 423.5 %all-reduce.7.cloned.1.call-start = ((), (), s32[]{:S(2)}) async-start(), calls=%async_computation.8 | async-start | bytes 524288 | tf_op jit(solution)/shard_map/psum | solution.py:27
  1949.9 149.1 %collective-permute-start.2 = (f32[6656,256]{0,1:T(8,128)}, f32[6656,256]{0,1:T(8,128)S(1)}, u32[]{:S(2)}, u32[]{:S(2)}) collective-permute-start(f32[6656,256]{0,1:T(8,128)} %convolution_bitcast_fusion.1), channel_id=1, source_target_pairs={{0,8},{8,0},{16,24},{24,16},{1,9},{9,1},{17,25},{25,17},{2,10},{10... | collective-permute-start | bytes 20447240 | tf_op jit(solution)/shard_map/ppermute | solution.py:45
  2103.0 148.2 %collective-permute-start.3 = (f32[6656,256]{0,1:T(8,128)S(1)}, f32[6656,256]{0,1:T(8,128)}, u32[]{:S(2)}, u32[]{:S(2)}) collective-permute-start(f32[6656,256]{0,1:T(8,128)S(1)} %add.49), channel_id=1, source_target_pairs={{0,16},{8,24},{16,0},{24,8},{1,17},{9,25},{17,1},{25,9},{2,18},{10... | collective-permute-start | bytes 20447240 | tf_op jit(solution)/shard_map/ppermute | solution.py:45
  2255.2 2.9 copy-start.2
  2264.4 204.9 %reduce-scatter.6.cloned.1.call-start = ((), (), s32[]{:S(2)}) async-start(), calls=%async_computation.9 | async-start | bytes 4718592 | tf_op jit(solution)/shard_map/reduce_scatter | solution.py:53
  2357.8 32.4 %slice-start.4 = ((s8[6815744]{0:T(1024)(128)(4,1)}), s8[2621440]{0:T(1024)(128)(4,1)S(1)}, s32[]{:S(2)}) async-start(s8[6815744]{0:T(1024)(128)(4,1)} %bitcast.126), calls=%async_computation.17 | async-start | bytes 5242880
  2381.6 8.7 slice-start.5
  2386.9 7.7 copy-start.6
  2420.1 79.0 %all-gather.8.cloned.1.call-start = ((), (), s32[]{:S(2)}) async-start(), calls=%async_computation.10 | async-start | bytes 2359296 | tf_op jit(solution)/shard_map/all_gather | solution.py:61
  2471.1 423.7 %all-reduce.9.cloned.1.call-start = ((), (), s32[]{:S(2)}) async-start(), calls=%async_computation.11 | async-start | bytes 524288 | tf_op jit(solution)/shard_map/psum | solution.py:27
  2525.2 149.1 %collective-permute-start.4 = (f32[6656,256]{0,1:T(8,128)}, f32[6656,256]{0,1:T(8,128)S(1)}, u32[]{:S(2)}, u32[]{:S(2)}) collective-permute-start(f32[6656,256]{0,1:T(8,128)} %convolution_bitcast_fusion), channel_id=1, source_target_pairs={{0,8},{8,0},{16,24},{24,16},{1,9},{9,1},{17,25},{25,17},{2,10},{10... | collective-permute-start | bytes 20447240 | tf_op jit(solution)/shard_map/ppermute | solution.py:45
  2678.3 148.2 %collective-permute-start.5 = (f32[6656,256]{0,1:T(8,128)S(1)}, f32[6656,256]{0,1:T(8,128)}, u32[]{:S(2)}, u32[]{:S(2)}) collective-permute-start(f32[6656,256]{0,1:T(8,128)S(1)} %add.51), channel_id=1, source_target_pairs={{0,16},{8,24},{16,0},{24,8},{1,17},{9,25},{17,1},{25,9},{2,18},{10... | collective-permute-start | bytes 20447240 | tf_op jit(solution)/shard_map/ppermute | solution.py:45
  2830.5 2.9 copy-start.1
  2839.8 206.2 %reduce-scatter.8.cloned.1.call-start = ((), (), s32[]{:S(2)}) async-start(), calls=%async_computation.12 | async-start | bytes 4718592 | tf_op jit(solution)/shard_map/reduce_scatter | solution.py:53
  2933.2 32.4 %slice-start.2 = ((s8[6815744]{0:T(1024)(128)(4,1)}), s8[2621440]{0:T(1024)(128)(4,1)S(1)}, s32[]{:S(2)}) async-start(s8[6815744]{0:T(1024)(128)(4,1)} %bitcast.124), calls=%async_computation.15 | async-start | bytes 5242880
  2956.9 8.7 slice-start.3
  2962.3 8.5 copy-start.3
  2996.8 2.0 copy-start.4
Sparse Core Ops, SparseCore 0:
  88.9 49.5 all-gather.3
  1687.2 55.3 all-reduce.4
  1845.1 48.9 reduce-scatter.3
  1896.2 27.6 all-gather.5
  2264.5 54.8 all-reduce.6
  2420.3 48.9 reduce-scatter.5
  2471.5 27.5 all-gather.7
  2839.9 54.8 all-reduce.8
  2997.0 48.9 reduce-scatter.7
